TPU v7x, 128 devices: a whole 4x4x4 slice. The times are simulated.
128 devices in a mesh: dp: 16 (over x, y), feat: 8 (over z, core).
Axes of the slice: x: 4, y: 4, z: 4, core: 2. Of those that a mesh axis runs over, the one named last changes fastest.
Arguments:
- images: bfloat16 [8192, 3072], P(('dp', 'feat')), may hold values from -6 to 6
- labels: int32 [8192], P('dp'), may hold values from 0 to 999
- predictions: float32 [8192, 1000], P('dp'), may hold values from -2 to 2
- filters: bfloat16 [75, 1024], P(None, 'feat'), may hold values from -0.75 to 0.75
- biases: float32 [1024], P('feat'), may hold values from -3 to 3
Outputs:
- weights: float32 [4096, 1000], P('feat')
- new_residual: float32 [8192, 1000], P(('dp', 'feat'))
All inputs are finite; a program needn't handle non-finite values.
Results may differ from a plain program's by a relative error of at most 0.007.
The roundings to bfloat16 on the way count: a program that leaves them out, or rounds other values in their place, can miss the bound.
Values may be sent and summed in bfloat16 or wider, within the bound.
No kernel may reach another device: no remote copies, remote signals or barrier semaphores. Data moves between devices by JAX's collectives and lax.ppermute only.
A program may use at most 192 MiB of HBM per device.

v0:
```python
import math
import jax
import jax.numpy as jnp
from jax import lax
from jax.sharding import PartitionSpec as P

SIDE = 32
CHAN = 3
KSIZE = 5


def chol_solve(factor, rhs):
    middle = lax.linalg.triangular_solve(factor, rhs, left_side=True, lower=True, transpose_a=False)
    return lax.linalg.triangular_solve(factor, middle, left_side=True, lower=True, transpose_a=True)


def split_parts(values):
    upper = values.astype(jnp.bfloat16)
    lower = (values - upper.astype(jnp.float32)).astype(jnp.bfloat16)
    return (upper, lower)


def left_product(feats, other):
    return lax.dot_general(
        feats, other, (((0,), (0,)), ((), ())), preferred_element_type=jnp.float32
    )


def conv_pool(imgs, kernel, offsets):
    count = imgs.shape[0]
    filt_count = kernel.shape[3]
    pics = imgs.reshape(count, SIDE, SIDE, CHAN)
    response = lax.conv_general_dilated(
        pics,
        kernel,
        (1, 1),
        "VALID",
        dimension_numbers=("NHWC", "HWIO", "NHWC"),
        preferred_element_type=jnp.float32,
    )
    response = jnp.maximum(response + offsets, 0.0)
    half = (SIDE - KSIZE + 1) // 2
    pooled = response.reshape(count, 2, half, 2, half, filt_count).mean(axis=(2, 4))
    return jnp.transpose(pooled, (0, 3, 1, 2)).reshape(count, 4 * filt_count).astype(jnp.bfloat16)


def shards(images, labels, predictions, filters, biases):
    filt_count = filters.shape[1]
    kernel = filters.reshape(KSIZE, KSIZE, CHAN, filt_count)
    share = images.shape[0]
    total_images = share * lax.axis_size("feat") * lax.axis_size("dp")
    piece = lax.all_gather(images, "feat", axis=0, tiled=True)
    count = piece.shape[0]
    group = math.gcd(count, 128)
    blocks = piece.reshape(count // group, group, piece.shape[1])
    out = lax.map(lambda part: conv_pool(part, kernel, biases), blocks)
    feats = out.reshape(count, 4 * filt_count)
    width = feats.shape[1]
    residual = (
        labels[:, None] == jnp.arange(predictions.shape[1], dtype=jnp.int32)[None, :]
    ).astype(jnp.float32) - predictions
    res_upper, res_lower = split_parts(residual)
    gram = lax.psum(left_product(feats, feats), "dp")
    cross = left_product(feats, res_upper) + left_product(feats, res_lower)
    cross, gram = lax.optimization_barrier((cross, gram))
    cross = lax.psum(cross, "dp")
    gram = gram / total_images + 0.5 * jnp.eye(width, dtype=jnp.float32)
    cross = cross / total_images
    factor = jnp.linalg.cholesky(gram)
    solved = chol_solve(factor, cross)
    sol_upper, sol_lower = split_parts(solved)
    fitted = lax.psum_scatter(
        (
            jnp.dot(feats, sol_upper, preferred_element_type=jnp.float32)
            + jnp.dot(feats, sol_lower, preferred_element_type=jnp.float32)
        ).astype(jnp.bfloat16),
        "feat",
        scatter_dimension=0,
        tiled=True,
    ).astype(jnp.float32)
    mine = lax.dynamic_slice_in_dim(residual, lax.axis_index("feat") * share, share, 0)
    return (solved, mine - fitted)


def solution(mesh):
    placed = (P(("dp", "feat"), None), P("dp"), P("dp", None), P(None, "feat"), P("feat"))
    return jax.shard_map(
        shards,
        mesh=mesh,
        in_specs=placed,
        out_specs=(P("feat", None), P(("dp", "feat"), None)),
        check_vma=False,
    )
```

profile of v0, /device:TPU:0, one launch (start us, length us, event | category | flops | bytes accessed | tf_op | source)
XLA Modules:
  0.0 528.2 jit_solution(10686514619989856401)
XLA Ops:
  8.0 0.7 reshape.78
  8.7 2.9 copy.22
  12.1 28.0 %all-gather.2.cloned.1.call-done = bf16[512,3072]{1,0:T(8,128)(2,1)} async-done(((bf16[64,3072]{1,0:T(8,128)(2,1)}), bf16[512,3072]{1,0:T(8,128)(2,1)}) %all-gather.2.cloned.1.call-update) | async-done | bytes 3145744 | tf_op jit(solution)/shard_map/all_gather | solution.py:52
  40.1 152.3 %while.11 = (s32[]{:T(128)}, bf16[4,128,512]{1,2,0:T(8,128)(2,1)}, bf16[4,128,3072]{2,1,0:T(8,128)(2,1)}, bf16[5,5,3,128]{3,2,1,0:T(4,128)(2,1)S(1)}, f32[128]{0:T(128)S(1)}, /*index=5*/s32[]{:T(128)}, f32[]{:T(128)}) while((s32[]{:T(128)}, bf16[4,128,512]{1,2,0:T(8,128)(2,1)}, bf16[4,128,3072]{2,1,0:T(8,128)(2,1)}, ...), condition=%wide.region_2.3_spmd, body=%wide.region_0.2_spmd.sunk | while | flops 1965359104 | bytes 109465424 | solution.py:56
  40.1 1.2 constant_dynamic-slice_fusion.4
  42.1 19.1 %add_maximum_fusion.2 = f32[128,28,28,128]{3,0,2,1:T(8,128)} fusion(f32[128]{0:T(128)S(1)} %get-tuple-element.169, bf16[128,32,32,3]{0,3,2,1:T(4,128)(2,1)S(1)} %reshape.101, bf16[5,5,3,128]{3,2,1,0:T(4,128)(2,1)S(1)} %get-tuple-element.168), kind=kOutput, calls=%fused_computation.clone.1 | convolution fusion | flops 1952448512 | bytes 52186368 | tf_op jit(solution)/shard_map/while/body/eval_jaxpr/conv_general_dilated | solution.py:33
  61.2 16.1 %reduce_sum.10 = f32[128,2,2,128]{3,0,2,1:T(8,128)S(1)} reduce(f32[128,2,14,2,14,128]{5,0,4,3,2,1:T(8,128)} %bitcast.85, f32[]{:T(128)} %constant.173.clone.1..sunk), dimensions={2,4}, to_apply=%region_1.1 | reduce | flops 12779520 | bytes 51642372 | tf_op jit(solution)/shard_map/while/body/eval_jaxpr/reduce_sum | solution.py:43
  78.2 1.2 constant_dynamic-slice_fusion.4
  80.1 19.1 %add_maximum_fusion.2 = f32[128,28,28,128]{3,0,2,1:T(8,128)} fusion(f32[128]{0:T(128)S(1)} %get-tuple-element.169, bf16[128,32,32,3]{0,3,2,1:T(4,128)(2,1)S(1)} %reshape.101, bf16[5,5,3,128]{3,2,1,0:T(4,128)(2,1)S(1)} %get-tuple-element.168), kind=kOutput, calls=%fused_computation.clone.1 | convolution fusion | flops 1952448512 | bytes 52186368 | tf_op jit(solution)/shard_map/while/body/eval_jaxpr/conv_general_dilated | solution.py:33
  99.3 16.1 %reduce_sum.10 = f32[128,2,2,128]{3,0,2,1:T(8,128)S(1)} reduce(f32[128,2,14,2,14,128]{5,0,4,3,2,1:T(8,128)} %bitcast.85, f32[]{:T(128)} %constant.173.clone.1..sunk), dimensions={2,4}, to_apply=%region_1.1 | reduce | flops 12779520 | bytes 51642372 | tf_op jit(solution)/shard_map/while/body/eval_jaxpr/reduce_sum | solution.py:43
  116.2 1.2 constant_dynamic-slice_fusion.4
  118.2 19.1 %add_maximum_fusion.2 = f32[128,28,28,128]{3,0,2,1:T(8,128)} fusion(f32[128]{0:T(128)S(1)} %get-tuple-element.169, bf16[128,32,32,3]{0,3,2,1:T(4,128)(2,1)S(1)} %reshape.101, bf16[5,5,3,128]{3,2,1,0:T(4,128)(2,1)S(1)} %get-tuple-element.168), kind=kOutput, calls=%fused_computation.clone.1 | convolution fusion | flops 1952448512 | bytes 52186368 | tf_op jit(solution)/shard_map/while/body/eval_jaxpr/conv_general_dilated | solution.py:33
  137.3 16.1 %reduce_sum.10 = f32[128,2,2,128]{3,0,2,1:T(8,128)S(1)} reduce(f32[128,2,14,2,14,128]{5,0,4,3,2,1:T(8,128)} %bitcast.85, f32[]{:T(128)} %constant.173.clone.1..sunk), dimensions={2,4}, to_apply=%region_1.1 | reduce | flops 12779520 | bytes 51642372 | tf_op jit(solution)/shard_map/while/body/eval_jaxpr/reduce_sum | solution.py:43
  154.3 1.2 constant_dynamic-slice_fusion.4
  156.3 19.1 %add_maximum_fusion.2 = f32[128,28,28,128]{3,0,2,1:T(8,128)} fusion(f32[128]{0:T(128)S(1)} %get-tuple-element.169, bf16[128,32,32,3]{0,3,2,1:T(4,128)(2,1)S(1)} %reshape.101, bf16[5,5,3,128]{3,2,1,0:T(4,128)(2,1)S(1)} %get-tuple-element.168), kind=kOutput, calls=%fused_computation.clone.1 | convolution fusion | flops 1952448512 | bytes 52186368 | tf_op jit(solution)/shard_map/while/body/eval_jaxpr/conv_general_dilated | solution.py:33
  175.4 16.1 %reduce_sum.10 = f32[128,2,2,128]{3,0,2,1:T(8,128)S(1)} reduce(f32[128,2,14,2,14,128]{5,0,4,3,2,1:T(8,128)} %bitcast.85, f32[]{:T(128)} %constant.173.clone.1..sunk), dimensions={2,4}, to_apply=%region_1.1 | reduce | flops 12779520 | bytes 51642372 | tf_op jit(solution)/shard_map/while/body/eval_jaxpr/reduce_sum | solution.py:43
  192.4 2.7 convolution_bitcast_fusion
  195.4 1.9 convert_subtract_fusion
  198.2 2.0 convolution_add_fusion
  200.3 82.0 %all-reduce.4.cloned.1.call-done = f32[512,512]{1,0:T(8,128)} async-done(((f32[512,512]{1,0:T(8,128)}), f32[512,512]{1,0:T(8,128)}) %all-reduce.4.cloned.1.call-update) | async-done | bytes 1048592 | tf_op jit(solution)/shard_map/psum | solution.py:63
  282.3 2.3 select_add_fusion
  284.6 2.6 copy.24
  287.2 1.8 fusion.19
  289.0 1.0 copy-done.3
  290.0 11.7 %cholesky.103 = f32[128,128]{1,0:T(8,128)S(1)} custom-call(f32[128,128]{1,0:T(8,128)S(1)} %cholesky.263), custom_call_target="Cholesky" | custom-call | tf_op jit(solution)/shard_map/jit(cholesky)/cholesky | solution.py:69
  301.7 1.1 cholesky.222
  302.8 9.8 %custom-call.32 = f32[1,128,128]{1,2,0:T(8,128)S(1)} custom-call(f32[1,128,128]{2,1,0:T(8,128)S(1)} %get-tuple-element.86), custom_call_target="InvertDiagBlocksLowerTriangular" | custom-call | tf_op jit(solution)/shard_map/jit(cholesky)/cholesky | solution.py:69
  312.6 2.0 constant_dynamic-update-slice_fusion.4
  314.6 1.3 convolution_subtract_fusion.4
  315.9 12.1 %cholesky.215 = f32[128,128]{1,0:T(8,128)S(1)} custom-call(f32[128,128]{1,0:T(8,128)S(1)} %cholesky.267), custom_call_target="Cholesky" | custom-call | tf_op jit(solution)/shard_map/jit(cholesky)/cholesky | solution.py:69
  328.6 9.8 %custom-call.33 = f32[1,128,128]{1,2,0:T(8,128)S(1)} custom-call(f32[1,128,128]{2,1,0:T(8,128)S(1)} %get-tuple-element.83), custom_call_target="InvertDiagBlocksLowerTriangular" | custom-call | tf_op jit(solution)/shard_map/jit(cholesky)/cholesky | solution.py:69
  338.4 0.9 convolution_dynamic-update-slice_fusion
  339.4 1.4 convolution_subtract_fusion.5
  340.8 11.7 %cholesky.236 = f32[128,128]{1,0:T(8,128)S(1)} custom-call(f32[128,128]{1,0:T(8,128)S(1)} %cholesky.272), custom_call_target="Cholesky" | custom-call | tf_op jit(solution)/shard_map/jit(cholesky)/cholesky | solution.py:69
  353.1 9.8 %custom-call.34 = f32[1,128,128]{1,2,0:T(8,128)S(1)} custom-call(f32[1,128,128]{2,1,0:T(8,128)S(1)} %get-tuple-element.80), custom_call_target="InvertDiagBlocksLowerTriangular" | custom-call | tf_op jit(solution)/shard_map/jit(cholesky)/cholesky | solution.py:69
  363.0 0.8 convolution_dynamic-update-slice_fusion.1
  363.8 1.4 convolution_subtract_fusion.6
  365.2 11.9 %cholesky.253 = f32[128,128]{1,0:T(8,128)S(1)} custom-call(f32[128,128]{1,0:T(8,128)S(1)} %convolution_subtract_fusion.6), custom_call_target="Cholesky" | custom-call | tf_op jit(solution)/shard_map/jit(cholesky)/cholesky | solution.py:69
  382.1 2.3 select_select_fusion
  384.4 14.6 %while.12 = (s32[]{:T(128)}, f32[512,512]{1,0:T(8,128)}, s32[4,2]{0,1:T(2,128)S(1)}, f32[4,128,128]{2,1,0:T(8,128)}, s32[]{:T(128)}) while((s32[]{:T(128)}, f32[512,512]{1,0:T(8,128)}, s32[4,2]{0,1:T(2,128)S(1)}, f32[4,128,128]{2,1,0:T(8,128)}, s32[]{:T(128)}) %tuple.52), condition=%wide.while_cond, body=%wide.while_body.sunk | while | flops 2 | bytes 132705 | solution.py:14
  385.1 3.0 bitcast_dynamic-update-slice_fusion.2
  388.7 3.0 bitcast_dynamic-update-slice_fusion.2
  392.4 3.0 bitcast_dynamic-update-slice_fusion.2
  396.1 2.9 bitcast_dynamic-update-slice_fusion.2
  399.0 40.1 %custom-call.35 = f32[4,128,128]{1,2,0:T(8,128)S(1)} custom-call(f32[4,128,128]{2,1,0:T(8,128)} %get-tuple-element.41), custom_call_target="InvertDiagBlocksLowerTriangular" | custom-call | tf_op jit(solution)/shard_map/triangular_solve | solution.py:14
  439.1 28.5 %all-reduce.6.cloned.1.call-done = f32[512,1000]{0,1:T(8,128)} async-done(((f32[512,1000]{0,1:T(8,128)}), f32[512,1000]{0,1:T(8,128)}) %all-reduce.6.cloned.1.call-update) | async-done | bytes 2048016 | tf_op jit(solution)/shard_map/psum | solution.py:66
  467.6 1.9 broadcast_multiply_fusion
  469.5 0.9 fusion.29
  470.5 1.0 convolution_subtract_fusion.3
  471.5 1.0 fusion.53
  472.4 1.0 convolution_subtract_fusion.1
  473.4 0.9 fusion.55
  474.4 1.8 fusion.16
  476.1 1.0 fusion.57
  477.1 1.0 fusion.56
  478.1 1.0 convolution_subtract_fusion.2
  479.0 1.0 fusion.54
  480.0 1.0 convolution_subtract_fusion
  481.0 1.2 fusion.52
  482.2 1.8 fusion.13
  484.0 1.0 fusion.51
  486.4 1.7 add_convert_fusion
  488.2 31.7 %reduce-scatter.2.cloned.1.call-done = bf16[64,1000]{1,0:T(8,128)(2,1)} async-done(((bf16[512,1000]{1,0:T(8,128)(2,1)}), bf16[64,1000]{1,0:T(8,128)(2,1)}) %reduce-scatter.2.cloned.1.call-update) | async-done | bytes 128016 | tf_op jit(solution)/shard_map/reduce_scatter | solution.py:72
  519.8 1.6 convert_subtract_fusion.1
  (67 shorter events, 16.9 us)
Async XLA Ops:
  7.2 32.9 %all-gather.2.cloned.1.call-start = ((), (), s32[]{:S(2)}) async-start(), calls=%async_computation.1 | async-start | bytes 3538944 | tf_op jit(solution)/shard_map/all_gather | solution.py:52
  7.9 274.4 %all-reduce.4.cloned.1.call-start = ((), (), s32[]{:S(2)}) async-start(), calls=%async_computation.2 | async-start | bytes 2097152 | tf_op jit(solution)/shard_map/psum | solution.py:63
  8.7 31.4 %copy-start.5 = (f32[128]{0:T(128)S(1)}, f32[128]{0:T(128)}, u32[]{:S(2)}) copy-start(f32[128]{0:T(128)} %param.11) | copy-start | bytes 1540
  192.4 3.0 copy-start.4
  195.1 2.1 copy-start.1
  195.1 272.5 %all-reduce.6.cloned.1.call-start = ((), (), s32[]{:S(2)}) async-start(), calls=%async_computation.3 | async-start | bytes 4096000 | tf_op jit(solution)/shard_map/psum | solution.py:66
  289.0 1.0 copy-start.3
  377.1 7.3 %copy-start.6 = (s32[4]{0:T(128)S(1)}, s32[4]{0:T(128)}, u32[]{:S(2)}) copy-start(s32[4]{0:T(128)} %iota_multiply_fusion) | copy-start | bytes 52
  377.1 142.7 %reduce-scatter.2.cloned.1.call-start = ((), (), s32[]{:S(2)}) async-start(), calls=%async_computation.4 | async-start | bytes 1179648 | tf_op jit(solution)/shard_map/reduce_scatter | solution.py:72
  467.6 2.8 copy-start.2
  485.1 1.3 copy-start
Sparse Core Ops, SparseCore 0:
  9.7 30.3 all-gather.1
  195.2 86.9 all-reduce.3
  377.2 90.3 all-reduce.5
  488.3 31.4 reduce-scatter.1
where the time goes:
time: 533 us; the launch traced here: 528 us
  other arithmetic  198 us (37%)
  waiting for transfers between devices  171 us (32%)
  matrix products  108 us (20%)
  local copies, waits for them, and re-layouts  34.7 us (7%)
  between operations  16.6 us (3%)
    psum x1, waiting for transfers between devices, shards(): gram = lax.psum(left_product(feats, feats), 'dp')  82 us
    another operation x14, other arithmetic, shards(): factor = jnp.linalg.cholesky(gram)  80.7 us
    conv_general_dilated x4, matrix products, conv_pool(): lax.conv_general_dilated(pics, kernel, (1, 1), 'VALID', dimension_numbers...  76.5 us
    reduce_sum x4, other arithmetic, conv_pool(): response.reshape(count, 2, half, 2, half, filt_count).mean(axis=(2, 4))  64.5 us
    another operation x4, other arithmetic, chol_solve(): lax.linalg.triangular_solve(factor, middle, left_side=True, lower=True, t...  43.1 us
    reduce_scatter x1, waiting for transfers between devices, shards(): lax.psum_scatter((jnp.dot(feats, sol_upper, preferred_element_type=jnp.fl...  31.7 us
    psum x1, waiting for transfers between devices, shards(): cross = lax.psum(cross, 'dp')  28.5 us
    all_gather x1, waiting for transfers between devices, shards(): piece = lax.all_gather(images, 'feat', axis=0, tiled=True)  28 us
  transfers between devices with their start and end apart: 4, of which 4 were waited for; matrix products, arithmetic and copies ran while one was open for 13% of the time, Pallas kernels for 0%

commit v1 on v0

--- a/solution.py
+++ b/solution.py
@@ -63,7 +63,9 @@
     gram = lax.psum(left_product(feats, feats), "dp")
     cross = left_product(feats, res_upper) + left_product(feats, res_lower)
     cross, gram = lax.optimization_barrier((cross, gram))
-    cross = lax.psum(cross, "dp")
+    cross = cross
+    for hop in (1, 2, 4, 8):
+        cross = cross + lax.ppermute(cross, "dp", [(dev, dev ^ hop) for dev in range(16)])
     gram = gram / total_images + 0.5 * jnp.eye(width, dtype=jnp.float32)
     cross = cross / total_images
     factor = jnp.linalg.cholesky(gram)

time: 533 us -> 588 us (1.10)
  waiting for transfers between devices: 171 us -> 211 us
  other arithmetic: 198 us -> 209 us
    ppermute x0 -> x4, waiting for transfers between devices: none -> 67.9 us  [shards(): lax.ppermute(cross, 'dp', [(dev, dev ^ hop) for dev in range(16)])]
    psum x1 -> x0, waiting for transfers between devices: 28.5 us -> none  [shards(): cross = lax.psum(cross, 'dp')]
    add x0 -> x3, other arithmetic: none -> 11.2 us  [shards(): cross + lax.ppermute(cross, 'dp', [(dev, dev ^ hop) for dev in range(16)])]
  transfers between devices with their start and end apart: 4 -> 7, of which waited for: 4 -> 5; matrix products, arithmetic and copies ran while one was open for 13% -> 27% of each run, Pallas kernels for 0% -> 0%
where the time goes in v1:
time: 588 us; the launch traced here: 582 us
  waiting for transfers between devices  211 us (36%)
  other arithmetic  209 us (36%)
  matrix products  108 us (18%)
  local copies, waits for them, and re-layouts  32.1 us (5%)
  between operations  16.6 us (3%)
    psum x1, waiting for transfers between devices, shards(): gram = lax.psum(left_product(feats, feats), 'dp')  82.1 us
    another operation x14, other arithmetic, shards(): factor = jnp.linalg.cholesky(gram)  80.3 us
    conv_general_dilated x4, matrix products, conv_pool(): lax.conv_general_dilated(pics, kernel, (1, 1), 'VALID', dimension_numbers...  76.5 us
    ppermute x4, waiting for transfers between devices, shards(): lax.ppermute(cross, 'dp', [(dev, dev ^ hop) for dev in range(16)])  67.9 us
    reduce_sum x4, other arithmetic, conv_pool(): response.reshape(count, 2, half, 2, half, filt_count).mean(axis=(2, 4))  64.5 us
    another operation x4, other arithmetic, chol_solve(): lax.linalg.triangular_solve(factor, middle, left_side=True, lower=True, t...  42.2 us
    reduce_scatter x1, waiting for transfers between devices, shards(): lax.psum_scatter((jnp.dot(feats, sol_upper, preferred_element_type=jnp.fl...  31.4 us
    all_gather x1, waiting for transfers between devices, shards(): piece = lax.all_gather(images, 'feat', axis=0, tiled=True)  28.5 us
  transfers between devices with their start and end apart: 7, of which 5 were waited for; matrix products, arithmetic and copies ran while one was open for 27% of the time, Pallas kernels for 0%

profile of v1, /device:TPU:0, one launch (start us, length us, event | category | flops | bytes accessed | tf_op | source)
XLA Modules:
  0.0 581.6 jit_solution(14744795407004950508)
XLA Ops:
  8.7 2.9 copy.22
  11.6 28.5 %all-gather.2.cloned.1.call-done = bf16[512,3072]{1,0:T(8,128)(2,1)} async-done(((bf16[64,3072]{1,0:T(8,128)(2,1)}), bf16[512,3072]{1,0:T(8,128)(2,1)}) %all-gather.2.cloned.1.call-update) | async-done | bytes 3145744 | tf_op jit(solution)/shard_map/all_gather | solution.py:52
  40.1 152.3 %while.11 = (s32[]{:T(128)}, bf16[4,128,512]{1,2,0:T(8,128)(2,1)}, bf16[4,128,3072]{2,1,0:T(8,128)(2,1)}, bf16[5,5,3,128]{3,2,1,0:T(4,128)(2,1)S(1)}, f32[128]{0:T(128)S(1)}, /*index=5*/s32[]{:T(128)}, f32[]{:T(128)}) while((s32[]{:T(128)}, bf16[4,128,512]{1,2,0:T(8,128)(2,1)}, bf16[4,128,3072]{2,1,0:T(8,128)(2,1)}, ...), condition=%wide.region_2.3_spmd, body=%wide.region_0.2_spmd.sunk | while | flops 1965359104 | bytes 109465424 | solution.py:56
  40.1 1.2 constant_dynamic-slice_fusion.4
  42.1 19.1 %add_maximum_fusion.2 = f32[128,28,28,128]{3,0,2,1:T(8,128)} fusion(f32[128]{0:T(128)S(1)} %get-tuple-element.169, bf16[128,32,32,3]{0,3,2,1:T(4,128)(2,1)S(1)} %reshape.101, bf16[5,5,3,128]{3,2,1,0:T(4,128)(2,1)S(1)} %get-tuple-element.168), kind=kOutput, calls=%fused_computation.clone.1 | convolution fusion | flops 1952448512 | bytes 52186368 | tf_op jit(solution)/shard_map/while/body/eval_jaxpr/conv_general_dilated | solution.py:33
  61.2 16.1 %reduce_sum.10 = f32[128,2,2,128]{3,0,2,1:T(8,128)S(1)} reduce(f32[128,2,14,2,14,128]{5,0,4,3,2,1:T(8,128)} %bitcast.82, f32[]{:T(128)} %constant.173.clone.1..sunk), dimensions={2,4}, to_apply=%region_1.1 | reduce | flops 12779520 | bytes 51642372 | tf_op jit(solution)/shard_map/while/body/eval_jaxpr/reduce_sum | solution.py:43
  78.2 1.2 constant_dynamic-slice_fusion.4
  80.1 19.1 %add_maximum_fusion.2 = f32[128,28,28,128]{3,0,2,1:T(8,128)} fusion(f32[128]{0:T(128)S(1)} %get-tuple-element.169, bf16[128,32,32,3]{0,3,2,1:T(4,128)(2,1)S(1)} %reshape.101, bf16[5,5,3,128]{3,2,1,0:T(4,128)(2,1)S(1)} %get-tuple-element.168), kind=kOutput, calls=%fused_computation.clone.1 | convolution fusion | flops 1952448512 | bytes 52186368 | tf_op jit(solution)/shard_map/while/body/eval_jaxpr/conv_general_dilated | solution.py:33
  99.3 16.1 %reduce_sum.10 = f32[128,2,2,128]{3,0,2,1:T(8,128)S(1)} reduce(f32[128,2,14,2,14,128]{5,0,4,3,2,1:T(8,128)} %bitcast.82, f32[]{:T(128)} %constant.173.clone.1..sunk), dimensions={2,4}, to_apply=%region_1.1 | reduce | flops 12779520 | bytes 51642372 | tf_op jit(solution)/shard_map/while/body/eval_jaxpr/reduce_sum | solution.py:43
  116.2 1.2 constant_dynamic-slice_fusion.4
  118.2 19.1 %add_maximum_fusion.2 = f32[128,28,28,128]{3,0,2,1:T(8,128)} fusion(f32[128]{0:T(128)S(1)} %get-tuple-element.169, bf16[128,32,32,3]{0,3,2,1:T(4,128)(2,1)S(1)} %reshape.101, bf16[5,5,3,128]{3,2,1,0:T(4,128)(2,1)S(1)} %get-tuple-element.168), kind=kOutput, calls=%fused_computation.clone.1 | convolution fusion | flops 1952448512 | bytes 52186368 | tf_op jit(solution)/shard_map/while/body/eval_jaxpr/conv_general_dilated | solution.py:33
  137.3 16.1 %reduce_sum.10 = f32[128,2,2,128]{3,0,2,1:T(8,128)S(1)} reduce(f32[128,2,14,2,14,128]{5,0,4,3,2,1:T(8,128)} %bitcast.82, f32[]{:T(128)} %constant.173.clone.1..sunk), dimensions={2,4}, to_apply=%region_1.1 | reduce | flops 12779520 | bytes 51642372 | tf_op jit(solution)/shard_map/while/body/eval_jaxpr/reduce_sum | solution.py:43
  154.3 1.2 constant_dynamic-slice_fusion.4
  156.3 19.1 %add_maximum_fusion.2 = f32[128,28,28,128]{3,0,2,1:T(8,128)} fusion(f32[128]{0:T(128)S(1)} %get-tuple-element.169, bf16[128,32,32,3]{0,3,2,1:T(4,128)(2,1)S(1)} %reshape.101, bf16[5,5,3,128]{3,2,1,0:T(4,128)(2,1)S(1)} %get-tuple-element.168), kind=kOutput, calls=%fused_computation.clone.1 | convolution fusion | flops 1952448512 | bytes 52186368 | tf_op jit(solution)/shard_map/while/body/eval_jaxpr/conv_general_dilated | solution.py:33
  175.4 16.1 %reduce_sum.10 = f32[128,2,2,128]{3,0,2,1:T(8,128)S(1)} reduce(f32[128,2,14,2,14,128]{5,0,4,3,2,1:T(8,128)} %bitcast.82, f32[]{:T(128)} %constant.173.clone.1..sunk), dimensions={2,4}, to_apply=%region_1.1 | reduce | flops 12779520 | bytes 51642372 | tf_op jit(solution)/shard_map/while/body/eval_jaxpr/reduce_sum | solution.py:43
  192.4 2.7 convolution_bitcast_fusion
  195.1 1.9 convert_subtract_fusion
  198.0 2.0 convolution_add_fusion
  200.1 82.1 %all-reduce.3.cloned.1.call-done = f32[512,512]{1,0:T(8,128)} async-done(((f32[512,512]{1,0:T(8,128)}), f32[512,512]{1,0:T(8,128)}) %all-reduce.3.cloned.1.call-update) | async-done | bytes 1048592 | tf_op jit(solution)/shard_map/psum | solution.py:63
  283.1 44.1 %collective-permute-done = f32[512,1000]{0,1:T(8,128)S(1)} collective-permute-done((f32[512,1000]{0,1:T(8,128)}, f32[512,1000]{0,1:T(8,128)S(1)}, u32[]{:S(2)}, u32[]{:S(2)}) %collective-permute-start) | collective-permute-done | bytes 2048032 | tf_op jit(solution)/shard_map/ppermute | solution.py:68
  327.2 3.3 add.84
  330.5 2.0 collective-permute-start.1
  332.5 2.3 select_add_fusion
  334.8 2.5 copy.24
  337.4 1.8 fusion.16
  339.1 1.0 copy-done.3
  340.1 11.7 %cholesky.103 = f32[128,128]{1,0:T(8,128)S(1)} custom-call(f32[128,128]{1,0:T(8,128)S(1)} %cholesky.263), custom_call_target="Cholesky" | custom-call | tf_op jit(solution)/shard_map/jit(cholesky)/cholesky | solution.py:71
  351.8 1.1 cholesky.222
  353.0 23.8 %collective-permute-done.1 = f32[512,1000]{0,1:T(8,128)} collective-permute-done((f32[512,1000]{0,1:T(8,128)}, f32[512,1000]{0,1:T(8,128)}, u32[]{:S(2)}, u32[]{:S(2)}) %collective-permute-start.1) | collective-permute-done | bytes 2048032 | tf_op jit(solution)/shard_map/ppermute | solution.py:68
  376.7 4.0 add.85
  380.9 9.8 %custom-call.32 = f32[1,128,128]{1,2,0:T(8,128)S(1)} custom-call(f32[1,128,128]{2,1,0:T(8,128)S(1)} %get-tuple-element.86), custom_call_target="InvertDiagBlocksLowerTriangular" | custom-call | tf_op jit(solution)/shard_map/jit(cholesky)/cholesky | solution.py:71
  390.7 2.0 constant_dynamic-update-slice_fusion.4
  392.7 1.2 convolution_subtract_fusion.2
  394.0 11.7 %cholesky.215 = f32[128,128]{1,0:T(8,128)S(1)} custom-call(f32[128,128]{1,0:T(8,128)S(1)} %cholesky.267), custom_call_target="Cholesky" | custom-call | tf_op jit(solution)/shard_map/jit(cholesky)/cholesky | solution.py:71
  406.3 9.8 %custom-call.33 = f32[1,128,128]{1,2,0:T(8,128)S(1)} custom-call(f32[1,128,128]{2,1,0:T(8,128)S(1)} %get-tuple-element.83), custom_call_target="InvertDiagBlocksLowerTriangular" | custom-call | tf_op jit(solution)/shard_map/jit(cholesky)/cholesky | solution.py:71
  417.1 1.5 convolution_subtract_fusion.3
  418.6 11.9 %cholesky.236 = f32[128,128]{1,0:T(8,128)S(1)} custom-call(f32[128,128]{1,0:T(8,128)S(1)} %cholesky.272), custom_call_target="Cholesky" | custom-call | tf_op jit(solution)/shard_map/jit(cholesky)/cholesky | solution.py:71
  431.1 9.8 %custom-call.34 = f32[1,128,128]{1,2,0:T(8,128)S(1)} custom-call(f32[1,128,128]{2,1,0:T(8,128)S(1)} %get-tuple-element.80), custom_call_target="InvertDiagBlocksLowerTriangular" | custom-call | tf_op jit(solution)/shard_map/jit(cholesky)/cholesky | solution.py:71
  441.7 1.4 convolution_subtract_fusion.4
  443.2 11.7 %cholesky.253 = f32[128,128]{1,0:T(8,128)S(1)} custom-call(f32[128,128]{1,0:T(8,128)S(1)} %convolution_subtract_fusion.4), custom_call_target="Cholesky" | custom-call | tf_op jit(solution)/shard_map/jit(cholesky)/cholesky | solution.py:71
  456.8 4.0 add.86
  460.8 2.5 collective-permute-start.3
  466.2 2.3 select_select_fusion
  468.6 12.1 %while.12 = (s32[]{:T(128)}, f32[512,512]{1,0:T(8,128)}, s32[4,2]{0,1:T(2,128)S(1)}, f32[4,128,128]{2,1,0:T(8,128)S(1)}, s32[]{:T(128)}) while((s32[]{:T(128)}, f32[512,512]{1,0:T(8,128)}, s32[4,2]{0,1:T(2,128)S(1)}, f32[4,128,128]{2,1,0:T(8,128)S(1)}, s32[]{:T(128)}) %tuple.52), condition=%wide.while_cond, body=%wide.while_body.sunk | while | flops 2 | bytes 131181 | solution.py:14
  469.3 2.4 bitcast_dynamic-update-slice_fusion.2
  472.3 2.4 bitcast_dynamic-update-slice_fusion.2
  475.4 2.4 bitcast_dynamic-update-slice_fusion.2
  478.4 2.3 bitcast_dynamic-update-slice_fusion.2
  480.7 39.7 %custom-call.35 = f32[4,128,128]{1,2,0:T(8,128)S(1)} custom-call(f32[4,128,128]{2,1,0:T(8,128)S(1)} %get-tuple-element.41), custom_call_target="InvertDiagBlocksLowerTriangular" | custom-call | tf_op jit(solution)/shard_map/triangular_solve | solution.py:14
  520.5 2.8 add_multiply_fusion
  524.2 1.0 fusion.46
  525.2 1.0 fusion.29
  526.1 1.0 fusion.17
  528.1 1.8 fusion.1
  529.8 1.0 fusion.27
  530.8 1.0 fusion.56
  532.7 1.0 fusion.55
  533.7 1.2 convolution_subtract_fusion
  534.9 1.0 fusion.54
  535.9 1.8 fusion.13
  537.7 1.0 fusion.53
  540.1 1.7 add_convert_fusion
  541.8 31.4 %reduce-scatter.2.cloned.1.call-done = bf16[64,1000]{1,0:T(8,128)(2,1)} async-done(((bf16[512,1000]{1,0:T(8,128)(2,1)}), bf16[64,1000]{1,0:T(8,128)(2,1)}) %reduce-scatter.2.cloned.1.call-update) | async-done | bytes 128016 | tf_op jit(solution)/shard_map/reduce_scatter | solution.py:74
  573.2 1.6 convert_subtract_fusion.1
  (73 shorter events, 22.7 us)
Async XLA Ops:
  7.2 32.9 %all-gather.2.cloned.1.call-start = ((), (), s32[]{:S(2)}) async-start(), calls=%async_computation.1 | async-start | bytes 3538944 | tf_op jit(solution)/shard_map/all_gather | solution.py:52
  7.9 274.3 %all-reduce.3.cloned.1.call-start = ((), (), s32[]{:S(2)}) async-start(), calls=%async_computation.2 | async-start | bytes 2097152 | tf_op jit(solution)/shard_map/psum | solution.py:63
  8.7 31.4 %copy-start.5 = (f32[128]{0:T(128)S(1)}, f32[128]{0:T(128)}, u32[]{:S(2)}) copy-start(f32[128]{0:T(128)} %param.11) | copy-start | bytes 1540
  192.4 2.8 copy-start.4
  195.1 2.0 copy-start.1
  195.1 378.2 %reduce-scatter.2.cloned.1.call-start = ((), (), s32[]{:S(2)}) async-start(), calls=%async_computation.3 | async-start | bytes 1179648 | tf_op jit(solution)/shard_map/reduce_scatter | solution.py:74
  282.2 45.0 %collective-permute-start = (f32[512,1000]{0,1:T(8,128)}, f32[512,1000]{0,1:T(8,128)S(1)}, u32[]{:S(2)}, u32[]{:S(2)}) collective-permute-start(f32[512,1000]{0,1:T(8,128)} %convolution_add_fusion), channel_id=1, source_target_pairs={{0,8},{8,0},{16,24},{24,16},{32,40},{40,32},{48,56},{56,48},{64,72... | collective-permute-start | bytes 6144008 | tf_op jit(solution)/shard_map/ppermute | solution.py:68
  330.5 46.2 %collective-permute-start.1 = (f32[512,1000]{0,1:T(8,128)}, f32[512,1000]{0,1:T(8,128)}, u32[]{:S(2)}, u32[]{:S(2)}) collective-permute-start(f32[512,1000]{0,1:T(8,128)} %add.84), channel_id=1, source_target_pairs={{0,16},{8,24},{16,0},{24,8},{32,48},{40,56},{48,32},{56,40},{64,80... | collective-permute-start | bytes 6144008 | tf_op jit(solution)/shard_map/ppermute | solution.py:68
  339.1 1.0 copy-start.3
  380.7 76.1 %collective-permute-start.2 = (f32[512,1000]{0,1:T(8,128)}, f32[512,1000]{0,1:T(8,128)}, u32[]{:S(2)}, u32[]{:S(2)}) collective-permute-start(f32[512,1000]{0,1:T(8,128)} %add.85), channel_id=1, source_target_pairs={{0,32},{8,40},{16,48},{24,56},{32,0},{40,8},{48,16},{56,24},{64,96... | collective-permute-start | bytes 6144008 | tf_op jit(solution)/shard_map/ppermute | solution.py:68
  460.8 59.7 %collective-permute-start.3 = (f32[512,1000]{0,1:T(8,128)}, f32[512,1000]{0,1:T(8,128)}, u32[]{:S(2)}, u32[]{:S(2)}) collective-permute-start(f32[512,1000]{0,1:T(8,128)} %add.86), channel_id=1, source_target_pairs={{0,64},{8,72},{16,80},{24,88},{32,96},{40,104},{48,112},{56,120},{... | collective-permute-start | bytes 6144008 | tf_op jit(solution)/shard_map/ppermute | solution.py:68
  520.4 3.7 copy-start.2
  538.8 1.3 copy-start
Sparse Core Ops, SparseCore 0:
  9.7 30.3 all-gather.1
  195.2 86.9 all-reduce.2
  542.0 31.2 reduce-scatter.1
